TPU v7x, 32 devices: a whole 2x2x4 slice. The times are simulated.
32 devices in a mesh: dp: 8 (over z, x), fsdp: 4 (over y, core).
Axes of the slice: x: 2, y: 2, z: 4, core: 2. Of those that a mesh axis runs over, the one named last changes fastest.
Arguments:
- dec_hidden: bfloat16 [1024, 4096], P('dp'), may hold values from -18 to 18
- w_query: bfloat16 [4096, 2048], P(None, 'fsdp'), may hold values from -0.01171875 to 0.01171875
- enc_states: bfloat16 [2, 1536, 2048], P(None, 'dp', 'fsdp')
- w_out: bfloat16 [2048, 4096], P('fsdp'), may hold values from -0.5 to 0.5
- norm_gain: float32 [4096], replicated, may hold values from 0.25 to 1.75
- w_vocab: bfloat16 [4096, 16384], P(None, 'fsdp'), may hold values from -1 to 1
- enc_segment: int32 [1536], replicated, may hold values from 0 to 3, as said below
- dec_segment: int32 [1024], P('dp'), may hold values from 0 to 3, as said below
- seg_map: int32 [8, 4], replicated, may hold values from 0 to 31, as said below
- targets: int32 [1024], P('dp'), may hold values from 0 to 16383
- loss_mask: int32 [1024], P('dp'), may hold values from 0 to 1, as said below
Outputs:
- mean_loss: float32 [], replicated
- grad_hidden: bfloat16 [1024, 4096], P('dp', 'fsdp')
- grad_gain: float32 [4096], P('fsdp')
Inputs may be any that keep to these rules, and one draw needn't show every extreme that they name: `enc_segment`: each encoder row of 192 tokens holds 4 segments numbered in order, never falling, each nonempty and at most 80 tokens long; one segment of every row is exactly 80 long. `dec_segment`: each decoder row of 128 tokens holds 4 segments numbered in order, never falling, each nonempty and at most 56 tokens long; one segment of every row is exactly 56 long. seg_map[b, j] names the encoder segment (encoder row times 4 plus its number in that row) read by segment j of decoder row b. Every encoder segment is named exactly once. The encoder row read in column j is (b + o_j) mod 8, with offsets o_j that are the same for every decoder row and differ between columns; one of them is 4 and one is 7. The segments of one encoder row go to different decoder rows. `loss_mask`: the first token of every decoder row has mask 1.
All inputs are finite; a program needn't handle non-finite values.
Results may differ from a plain program's by a relative error of at most 0.0086.
Values may be sent and summed in bfloat16 or wider, within the bound.
No kernel may reach another device: no remote copies, remote signals or barrier semaphores. Data moves between devices by JAX's collectives and lax.ppermute only.
A program may use at most 128 MiB of HBM per device.

v0:
```python
import jax
import jax.numpy as jnp
from jax import lax
from jax.sharding import PartitionSpec as P

HEAD_DIM = 64


def joined(x, axis, combine):
    everything = jax.tree.map(lambda part: lax.all_gather(part, axis), x)
    leading = jax.tree.map(lambda part: part[0], everything)

    def turn(k, so_far):
        return combine(so_far, jax.tree.map(lambda part: part[k], everything))

    return lax.fori_loop(1, lax.axis_size(axis), turn, leading)


def merge_totals(first_set, second_set):
    larger = jnp.maximum(first_set[0], second_set[0])
    combined = first_set[1] * jnp.exp(first_set[0] - larger) + second_set[1] * jnp.exp(
        second_set[0] - larger
    )
    return (larger, combined, first_set[2] + second_set[2])


def attend(carry, block, block_ids, queries, sources):
    run_max, run_sum, run_acc = carry
    block_rows = block.shape[1]
    heads_here = queries.shape[1]
    keys_block = block[0].astype(jnp.float32).reshape(block_rows, heads_here, HEAD_DIM)
    values_block = block[1].astype(jnp.float32).reshape(block_rows, heads_here, HEAD_DIM)
    scores = jnp.einsum("ihd,jhd->hij", queries, keys_block)
    allowed = (sources[:, None] == block_ids[None, :])[None]
    new_max = jnp.maximum(run_max, jnp.max(jnp.where(allowed, scores, jnp.float32(-1e30)), 2))
    weights = jnp.where(allowed, jnp.exp(scores - new_max[:, :, None]), 0.0)
    run_sum = jnp.sum(weights, 2)
    run_acc = jnp.einsum("hij,jhd->hid", weights, values_block)
    return (new_max, run_sum, run_acc)


def body(
    dec_hidden,
    w_query,
    enc_states,
    w_out,
    norm_gain,
    w_vocab,
    enc_segment,
    dec_segment,
    seg_map,
    targets,
    loss_mask,
):
    dp_index = lax.axis_index("dp")
    fsdp_index = lax.axis_index("fsdp")
    dp_count = lax.axis_size("dp")
    dec_len, width = dec_hidden.shape
    enc_len = enc_states.shape[1]
    heads_here = w_query.shape[1] // HEAD_DIM
    segments = seg_map.shape[1]
    feature_count = width // lax.axis_size("fsdp")
    vocab_here = w_vocab.shape[1]
    map_row = lax.dynamic_index_in_dim(seg_map, dp_index, 0, keepdims=False)
    segment_picks = dec_segment[:, None] == jnp.arange(segments)[None, :]
    sources = jnp.sum(jnp.where(segment_picks, map_row[None, :], 0), 1)
    query_proj = jnp.dot(dec_hidden, w_query, preferred_element_type=jnp.float32).astype(
        jnp.bfloat16
    )
    queries = (
        lax.optimization_barrier(query_proj)
        .astype(jnp.float32)
        .reshape(dec_len, heads_here, HEAD_DIM)
    )
    start_state = (
        jnp.full((heads_here, dec_len), -1e30, jnp.float32),
        jnp.zeros((heads_here, dec_len), jnp.float32),
        jnp.zeros((heads_here, dec_len, HEAD_DIM), jnp.float32),
    )
    global_ids = jnp.arange(dp_count * enc_len) // enc_len * segments + enc_segment
    state = attend(
        start_state,
        lax.all_gather(enc_states, "dp", axis=1, tiled=True),
        global_ids,
        queries,
        sources,
    )
    run_max, run_sum, run_acc = state
    attended = (
        (run_acc / run_sum[:, :, None])
        .transpose(1, 0, 2)
        .reshape(dec_len, heads_here * HEAD_DIM)
        .astype(jnp.bfloat16)
    )
    feature_start = fsdp_index * feature_count
    gain_part = lax.dynamic_slice_in_dim(norm_gain, feature_start, feature_count, 0)
    summed_full = lax.psum(
        jnp.dot(attended, w_out, preferred_element_type=jnp.float32), "fsdp"
    ) + dec_hidden.astype(jnp.float32)
    inv_root = lax.rsqrt(jnp.sum(summed_full * summed_full, 1) / width + 1e-06)
    unit_full = summed_full * inv_root[:, None]
    normed_full = (unit_full * norm_gain).astype(jnp.bfloat16)
    logits = jnp.dot(normed_full, w_vocab, preferred_element_type=jnp.float32)
    unit_part = lax.dynamic_slice_in_dim(unit_full, feature_start, feature_count, 1)
    local_target = targets - fsdp_index * vocab_here
    picked = jnp.arange(vocab_here)[None, :] == local_target[:, None]
    local_top = jnp.max(logits, 1)
    local_total = jnp.sum(jnp.exp(logits - local_top[:, None]), 1)
    local_pick = jnp.sum(jnp.where(picked, logits, 0.0), 1)
    row_top, row_total, target_logit = joined(
        (local_top, local_total, local_pick), "fsdp", merge_totals
    )
    log_total = row_top + jnp.log(row_total)
    mask_float = loss_mask.astype(jnp.float32)
    grad_logits = (
        mask_float[:, None] * (jnp.exp(logits - log_total[:, None]) - picked.astype(jnp.float32))
    ).astype(jnp.bfloat16)
    grad_normed = lax.psum_scatter(
        lax.dot_general(
            w_vocab, grad_logits, (((1,), (1,)), ((), ())), preferred_element_type=jnp.float32
        ),
        "fsdp",
        scatter_dimension=0,
        tiled=True,
    ).T
    grad_unit = grad_normed * gain_part
    inner_total = lax.psum(jnp.sum(grad_unit * unit_part, 1), "fsdp")
    grad_summed = inv_root[:, None] * (grad_unit - unit_part * (inner_total / width)[:, None])
    gain_local = jnp.sum(grad_normed * unit_part, 0)
    token_count, loss_total, gain_total = lax.psum(
        (jnp.sum(mask_float), jnp.sum(mask_float * (log_total - target_logit)), gain_local), "dp"
    )
    return (
        loss_total / token_count,
        (grad_summed / token_count).astype(jnp.bfloat16),
        gain_total / token_count,
    )


def solution(mesh):
    in_specs = (
        P("dp", None),
        P(None, "fsdp"),
        P(None, "dp", "fsdp"),
        P("fsdp", None),
        P(),
        P(None, "fsdp"),
        P(),
        P("dp"),
        P(),
        P("dp"),
        P("dp"),
    )
    out_specs = (P(), P("dp", "fsdp"), P("fsdp"))
    return jax.shard_map(body, mesh=mesh, in_specs=in_specs, out_specs=out_specs, check_vma=False)
```

profile of v0, /device:TPU:0, one launch (start us, length us, event | category | flops | bytes accessed | tf_op | source)
XLA Modules:
  0.0 266.7 jit_solution(12701368455562883856)
XLA Ops:
  7.2 0.7 all-gather.8.cloned.1.call-update
  8.0 3.2 %convolution_convert_fusion = bf16[128,512]{1,0:T(8,128)(2,1)S(1)} fusion(bf16[128,4096]{1,0:T(8,128)(2,1)} %param.13, bf16[4096,512]{1,0:T(8,128)(2,1)} %param.14), kind=kOutput, calls=%fused_computation.27 | convolution fusion | flops 536936448 | bytes 5373952 | tf_op jit(solution)/shard_map/dot_general | solution.py:67
  11.4 0.2 dynamic-slice_reduce_fusion
  11.7 0.2 broadcast_compare_fusion
  11.8 61.6 %all-gather.8.cloned.1.call-done = bf16[2,1536,512]{2,1,0:T(8,128)(2,1)} async-done(((bf16[2,192,512]{2,1,0:T(8,128)(2,1)}), bf16[2,1536,512]{2,1,0:T(8,128)(2,1)}) %all-gather.8.cloned.1.call-update) | async-done | bytes 3145744 | tf_op jit(solution)/shard_map/all_gather | solution.py:83
  73.4 3.2 %fusion.29 = (bf16[1,1536,512]{2,1,0:T(8,128)(2,1)}, bf16[1,1536,512]{2,1,0:T(8,128)(2,1)S(1)}) fusion(bf16[2,1536,512]{2,1,0:T(8,128)(2,1)} %all-gather.8.cloned.1.call-done), kind=kLoop, calls=%fused_computation.65 | loop fusion | bytes 6291456 | tf_op jit(solution)/shard_map/slice | solution.py:31
  76.6 1.7 copy.24
  78.3 3.8 %select_reduce_fusion = (f32[8,128]{1,0:T(8,128)S(1)}, f32[8,128,1536]{2,1,0:T(8,128)}) fusion(pred[128,1536]{1,0:T(8,128)(4,1)S(1)} %broadcast_compare_fusion, bf16[128,8,64]{0,2,1:T(8,128)(2,1)S(1)} %bitcast.64, bf16[1536,8,64]{0,2,1:T(8,128)(2,1)S(1)} %bitcast.62), kind=kOutput, calls=%fused_computation.11 | convolution fusion | flops 204471296 | bytes 8196096 | tf_op jit(solution)/shard_map/ihd,jhd->hij/dot_general | solution.py:33
  82.1 0.7 copy.25
  82.9 4.3 %fusion.7 = f32[8,128]{1,0:T(8,128)S(1)} fusion(f32[8,128,1536]{2,1,0:T(8,128)} %get-tuple-element.214, f32[8,128]{1,0:T(8,128)S(1)} %broadcast_maximum_fusion, pred[128,1536]{1,0:T(8,128)(4,1)S(1)} %broadcast_compare_fusion), kind=kLoop, calls=%fused_computation.12 | loop fusion | flops 4717568 | bytes 6496256 | tf_op jit(solution)/shard_map/reduce_sum | solution.py:37
  87.1 0.3 copy-done.2
  87.5 1.4 fusion.15
  88.8 0.8 copy-done.7
  89.6 2.0 fusion.31
  91.8 0.6 copy-done.10
  92.3 49.5 %all-reduce.3.cloned.1.call-done = f32[128,4096]{1,0:T(8,128)} async-done(((f32[128,4096]{1,0:T(8,128)}), f32[128,4096]{1,0:T(8,128)}) %all-reduce.3.cloned.1.call-update) | async-done | bytes 2097168 | tf_op jit(solution)/shard_map/psum | solution.py:97
  141.9 2.1 multiply_reduce_fusion
  144.1 0.4 fusion.12
  144.5 0.3 copy-done.8
  144.8 13.7 %fusion.30 = (f32[128]{0:T(128)S(1)}, f32[128,4096]{1,0:T(8,128)S(1)}) fusion(bf16[4096,4096]{1,0:T(8,128)(2,1)} %param.18, f32[128,4096]{1,0:T(8,128)S(1)} %fusion.12, f32[4096]{0:T(1024)S(1)} %copy-done.8), kind=kOutput, calls=%fused_computation.66 | convolution fusion | flops 4296540160 | bytes 37765632 | tf_op jit(solution)/shard_map/dot_general | solution.py:103
  158.6 0.7 select_reduce_fusion.1
  159.3 5.0 %all-gather.5 = f32[4,1,128]{2,1,0:T(1,128)S(1)} all-gather(f32[1,1,128]{2,1,0:T(1,128)S(1)} %bitcast.72), channel_id=4, replica_groups=mesh['dp'=8,'fsdp'=4] {'fsdp'}, dimensions={0}, use_global_device_ids=true | all-gather | bytes 2560 | tf_op jit(solution)/shard_map/all_gather | solution.py:10
  164.3 5.0 %all-gather.4 = f32[4,1,128]{2,1,0:T(1,128)S(1)} all-gather(f32[1,1,128]{2,1,0:T(1,128)S(1)} %bitcast.71), channel_id=3, replica_groups=mesh['dp'=8,'fsdp'=4] {'fsdp'}, dimensions={0}, use_global_device_ids=true | all-gather | bytes 2560 | tf_op jit(solution)/shard_map/all_gather | solution.py:10
  169.3 5.2 %all-gather.3 = f32[4,1,128]{2,1,0:T(1,128)S(1)} all-gather(f32[1,1,128]{2,1,0:T(1,128)S(1)} %bitcast.69), channel_id=2, replica_groups=mesh['dp'=8,'fsdp'=4] {'fsdp'}, dimensions={0}, use_global_device_ids=true | all-gather | bytes 2560 | tf_op jit(solution)/shard_map/all_gather | solution.py:10
  174.7 0.6 convert_reduce_fusion
  175.3 17.3 %convolution_bitcast_fusion = f32[4096,128]{0,1:T(8,128)} fusion(bf16[4096,4096]{1,0:T(8,128)(2,1)} %param.18, f32[128,4096]{1,0:T(8,128)S(1)} %get-tuple-element.216, f32[128]{0:T(128)S(1)} %get-tuple-element.209, f32[128]{0:T(128)S(1)} %convert_element_type.30, s32[128]{0:T(128)S(1)} %broadcast_subtract_fusion), kind=kOutput, calls=%fused_computation.14 | convolution fusion | flops 4298113024 | bytes 37750272 | tf_op jit(solution)/shard_map/dot_general | solution.py:119
  192.6 31.7 %reduce-scatter.2.cloned.1.call-done = f32[1024,128]{0,1:T(8,128)} async-done(((f32[4096,128]{0,1:T(8,128)}), f32[1024,128]{0,1:T(8,128)}) %reduce-scatter.2.cloned.1.call-update) | async-done | bytes 524304 | tf_op jit(solution)/shard_map/reduce_scatter | solution.py:118
  224.3 1.2 fusion.21
  225.5 5.8 %psum.38 = f32[128]{0:T(128)S(1)} all-reduce(f32[128]{0:T(128)S(1)} %get-tuple-element.185), channel_id=1, replica_groups=mesh['dp'=8,'fsdp'=4] {'fsdp'}, use_global_device_ids=true, to_apply=%region_16.17 | all-reduce | flops 128 | bytes 1024 | tf_op jit(solution)/shard_map/psum | solution.py:127
  231.2 22.5 %all-reduce = (f32[]{:T(128)}, f32[]{:T(128)}, f32[1024]{0:T(1024)S(1)}) all-reduce(f32[]{:T(128)} %get-tuple-element.189, f32[]{:T(128)} %get-tuple-element.188, f32[1024]{0:T(1024)S(1)} %get-tuple-element.184), channel_id=1, replica_groups=mesh['dp'=8,'fsdp'=4] {'dp'}, use_global_device_ids=true, to_apply=%region_11.12 | all-reduce | flops 1026 | bytes 8208 | tf_op jit(solution)/shard_map/psum | solution.py:130
  253.8 1.3 broadcast_divide_fusion
  256.4 2.6 divide_convert_fusion
  (43 shorter events, 0.7 us)
Async XLA Ops:
  7.2 4.2 %copy-start = (s32[8,4]{0,1:T(4,128)S(1)}, s32[8,4]{0,1:T(4,128)}, u32[]{:S(2)}) copy-start(s32[8,4]{0,1:T(4,128)} %param.21) | copy-start | bytes 388
  7.2 66.2 %all-gather.8.cloned.1.call-start = ((), (), s32[]{:S(2)}) async-start(), calls=%async_computation.1 | async-start | bytes 3538944 | tf_op jit(solution)/shard_map/all_gather | solution.py:83
  7.9 133.9 %all-reduce.3.cloned.1.call-start = ((), (), s32[]{:S(2)}) async-start(), calls=%async_computation.2 | async-start | bytes 4194304 | tf_op jit(solution)/shard_map/psum | solution.py:97
  8.0 3.6 %copy-start.11 = (s32[128]{0:T(128)S(1)}, s32[128]{0:T(128)}, u32[]{:S(2)}) copy-start(s32[128]{0:T(128)} %param.20) | copy-start | bytes 1540
  8.0 3.7 %copy-start.9 = (s32[1536]{0:T(1024)S(1)}, s32[1536]{0:T(1024)}, u32[]{:S(2)}) copy-start(s32[1536]{0:T(1024)} %param.19) | copy-start | bytes 18436
  82.8 4.6 %copy-start.2 = (f32[8,128,1536]{2,1,0:T(8,128)S(1)}, f32[8,128,1536]{2,1,0:T(8,128)}, u32[]{:S(2)}) copy-start(f32[8,128,1536]{2,1,0:T(8,128)} %get-tuple-element.214) | copy-start | bytes 18874372
  87.4 2.2 copy-start.7
  91.7 0.7 copy-start.10
  91.7 0.7 copy-start.12
  91.7 50.2 %copy-start.5 = (bf16[128,4096]{1,0:T(8,128)(2,1)S(1)}, bf16[128,4096]{1,0:T(8,128)(2,1)}, u32[]{:S(2)}) copy-start(bf16[128,4096]{1,0:T(8,128)(2,1)} %param.13) | copy-start | bytes 3145732
  91.7 132.6 %reduce-scatter.2.cloned.1.call-start = ((), (), s32[]{:S(2)}) async-start(), calls=%async_computation.3 | async-start | bytes 2621440 | tf_op jit(solution)/shard_map/reduce_scatter | solution.py:118
  141.9 2.2 copy-start.6
  144.1 0.7 copy-start.8
  144.8 13.8 %copy-start.3 = (f32[128,4096]{1,0:T(8,128)}, f32[128,4096]{1,0:T(8,128)S(1)}, u32[]{:S(2)}) copy-start(f32[128,4096]{1,0:T(8,128)S(1)} %fusion.12) | copy-start | bytes 6291460
  192.6 31.7 %copy-start.4 = (f32[128,4096]{1,0:T(8,128)S(1)}, f32[128,4096]{1,0:T(8,128)}, u32[]{:S(2)}) copy-start(f32[128,4096]{1,0:T(8,128)} %copy-done.3) | copy-start | bytes 6291460
  192.6 66.5 %copy-start.1 = (s32[8,4]{0,1:T(4,128)S(1)}, s32[8,4]{0,1:T(4,128)}, u32[]{:S(2)}) copy-start(s32[8,4]{0,1:T(4,128)} %param.21) | copy-start | bytes 388
Sparse Core Ops, SparseCore 0:
  10.2 63.1 all-gather.7
  91.8 49.9 all-reduce.2
  192.7 31.5 reduce-scatter.1
where the time goes:
time: 267 us
  waiting for transfers between devices  143 us (54%)
  blocking collectives  43.5 us (16%)
  matrix products  41.5 us (16%)
  between operations  16.4 us (6%)
  other arithmetic  13.6 us (5%)
  local copies, waits for them, and re-layouts  8.11 us (3%)
    all_gather x1, waiting for transfers between devices, body(): lax.all_gather(enc_states, 'dp', axis=1, tiled=True)  61.6 us
    psum x1, waiting for transfers between devices, body(): lax.psum(jnp.dot(attended, w_out, preferred_element_type=jnp.float32), 'f...  49.5 us
    reduce_scatter x1, waiting for transfers between devices, body(): lax.psum_scatter(lax.dot_general(w_vocab, grad_logits, (((1,), (1,)), (()...  31.7 us
    psum x1, blocking collectives, body(): lax.psum((jnp.sum(mask_float), jnp.sum(mask_float * (log_total - target_l...  22.5 us
    dot_general x1, matrix products, body(): lax.dot_general(w_vocab, grad_logits, (((1,), (1,)), ((), ())), preferred...  17.3 us
    all_gather x3, blocking collectives, joined(): everything = jax.tree.map(lambda part: lax.all_gather(part, axis), x)  15.3 us
    dot_general x1, matrix products, body(): logits = jnp.dot(normed_full, w_vocab, preferred_element_type=jnp.float32)  13.7 us
    psum x1, blocking collectives, body(): inner_total = lax.psum(jnp.sum(grad_unit * unit_part, 1), 'fsdp')  5.75 us
  transfers between devices with their start and end apart: 3, of which 3 were waited for; matrix products, arithmetic and copies ran while one was open for 1% of the time, Pallas kernels for 0%

commit v1 on v0

--- a/solution.py
+++ b/solution.py
@@ -78,13 +78,22 @@
         jnp.zeros((heads_here, dec_len, HEAD_DIM), jnp.float32),
     )
     global_ids = jnp.arange(dp_count * enc_len) // enc_len * segments + enc_segment
-    state = attend(
-        start_state,
-        lax.all_gather(enc_states, "dp", axis=1, tiled=True),
-        global_ids,
-        queries,
-        sources,
-    )
+
+    def kinds_attach(array_dim, local):
+        peer_axis = "dp"
+        view_out, u_next = (lax.axis_size(peer_axis), lax.axis_index(peer_axis))
+        wide_out, block_next = (local, 1)
+        while block_next < view_out:
+            block_now = lax.ppermute(
+                wide_out, peer_axis, list(map(lambda num: (num, num ^ block_next), range(view_out)))
+            )
+            response = jnp.concatenate([wide_out, block_now], array_dim)
+            opened = jnp.concatenate([block_now, wide_out], array_dim)
+            wide_out = jnp.where(u_next & block_next == 0, response, opened)
+            block_next = 2 * block_next
+        return wide_out
+
+    state = attend(start_state, kinds_attach(1, enc_states), global_ids, queries, sources)
     run_max, run_sum, run_acc = state
     attended = (
         (run_acc / run_sum[:, :, None])

time: 267 us -> 310 us (1.16)
  waiting for transfers between devices: 143 us -> 173 us
  starting transfers between devices: 0.12 us -> 7.56 us
  other arithmetic: 13.6 us -> 19.7 us
    ppermute x0 -> x3, waiting for transfers between devices: none -> 89.6 us  [kinds_attach(): lax.ppermute(wide_out, peer_axis, list(map(lambda num: (num, num ^ block_...]
    all_gather x1 -> x0, waiting for transfers between devices: 61.6 us -> none  [body(): lax.all_gather(enc_states, 'dp', axis=1, tiled=True)]
    ppermute x0 -> x3, starting transfers between devices: none -> 7.48 us  [kinds_attach(): lax.ppermute(wide_out, peer_axis, list(map(lambda num: (num, num ^ block_...]
    select_n x0 -> x3, other arithmetic: none -> 6.14 us  [kinds_attach(): wide_out = jnp.where(u_next & block_next == 0, response, opened)]
  transfers between devices with their start and end apart: 3 -> 5, of which waited for: 3 -> 5; matrix products, arithmetic and copies ran while one was open for 1% -> 1% of each run, Pallas kernels for 0% -> 0%
where the time goes in v1:
time: 310 us; the launch traced here: 309 us
  waiting for transfers between devices  173 us (56%)
  blocking collectives  43.5 us (14%)
  matrix products  41.2 us (13%)
  other arithmetic  19.7 us (6%)
  between operations  16.7 us (5%)
  local copies, waits for them, and re-layouts  7.76 us (3%)
  starting transfers between devices  7.56 us (2%)
    ppermute x3, waiting for transfers between devices, kinds_attach(): lax.ppermute(wide_out, peer_axis, list(map(lambda num: (num, num ^ block_...  89.6 us
    psum x1, waiting for transfers between devices, body(): lax.psum(jnp.dot(attended, w_out, preferred_element_type=jnp.float32), 'f...  51.6 us
    reduce_scatter x1, waiting for transfers between devices, body(): lax.psum_scatter(lax.dot_general(w_vocab, grad_logits, (((1,), (1,)), (()...  31.7 us
    psum x1, blocking collectives, body(): lax.psum((jnp.sum(mask_float), jnp.sum(mask_float * (log_total - target_l...  22.5 us
    dot_general x1, matrix products, body(): lax.dot_general(w_vocab, grad_logits, (((1,), (1,)), ((), ())), preferred...  17.3 us
    all_gather x3, blocking collectives, joined(): everything = jax.tree.map(lambda part: lax.all_gather(part, axis), x)  15.3 us
    dot_general x1, matrix products, body(): logits = jnp.dot(normed_full, w_vocab, preferred_element_type=jnp.float32)  13.7 us
    ppermute x3, starting transfers between devices, kinds_attach(): lax.ppermute(wide_out, peer_axis, list(map(lambda num: (num, num ^ block_...  7.48 us
  transfers between devices with their start and end apart: 5, of which 5 were waited for; matrix products, arithmetic and copies ran while one was open for 1% of the time, Pallas kernels for 0%

profile of v1, /device:TPU:0, one launch (start us, length us, event | category | flops | bytes accessed | tf_op | source)
XLA Modules:
  0.0 309.4 jit_solution(2207517145337787555)
XLA Ops:
  7.2 3.0 collective-permute-start
  10.2 9.3 %collective-permute-done = bf16[2,192,512]{2,1,0:T(8,128)(2,1)S(1)} collective-permute-done((bf16[2,192,512]{2,1,0:T(8,128)(2,1)}, bf16[2,192,512]{2,1,0:T(8,128)(2,1)S(1)}, u32[]{:S(2)}, u32[]{:S(2)}) %collective-permute-start) | collective-permute-done | bytes 393248 | tf_op jit(solution)/shard_map/ppermute | solution.py:87
  19.6 1.4 maximum_select_fusion.2
  21.0 1.9 collective-permute-start.1
  22.9 17.0 %collective-permute-done.1 = bf16[2,384,512]{2,1,0:T(8,128)(2,1)} collective-permute-done((bf16[2,384,512]{2,1,0:T(8,128)(2,1)S(1)}, bf16[2,384,512]{2,1,0:T(8,128)(2,1)}, u32[]{:S(2)}, u32[]{:S(2)}) %collective-permute-start.1) | collective-permute-done | bytes 786464 | tf_op jit(solution)/shard_map/ppermute | solution.py:87
  39.9 1.9 maximum_select_fusion.1
  41.8 2.6 collective-permute-start.2
  44.4 3.0 convolution_convert_fusion
  48.0 63.2 %collective-permute-done.2 = bf16[2,768,512]{2,1,0:T(8,128)(2,1)} collective-permute-done((bf16[2,768,512]{2,1,0:T(8,128)(2,1)S(1)}, bf16[2,768,512]{2,1,0:T(8,128)(2,1)}, u32[]{:S(2)}, u32[]{:S(2)}) %collective-permute-start.2) | collective-permute-done | bytes 1572896 | tf_op jit(solution)/shard_map/ppermute | solution.py:87
  111.2 2.8 maximum_select_fusion
  114.0 1.9 fusion.29
  115.9 1.7 copy.24
  117.6 3.8 %select_reduce_fusion = (f32[8,128]{1,0:T(8,128)S(1)}, f32[8,128,1536]{2,1,0:T(8,128)}) fusion(pred[128,1536]{1,0:T(8,128)(4,1)S(1)} %broadcast_compare_fusion, bf16[128,8,64]{0,2,1:T(8,128)(2,1)S(1)} %bitcast.64, bf16[1536,8,64]{0,2,1:T(8,128)(2,1)S(1)} %bitcast.62), kind=kOutput, calls=%fused_computation.11 | convolution fusion | flops 204471296 | bytes 8196096 | tf_op jit(solution)/shard_map/ihd,jhd->hij/dot_general | solution.py:33
  121.4 1.7 copy.25
  123.2 4.3 %fusion.7 = f32[8,128]{1,0:T(8,128)S(1)} fusion(f32[8,128,1536]{2,1,0:T(8,128)} %get-tuple-element.214, f32[8,128]{1,0:T(8,128)S(1)} %broadcast_maximum_fusion, pred[128,1536]{1,0:T(8,128)(4,1)S(1)} %broadcast_compare_fusion), kind=kLoop, calls=%fused_computation.12 | loop fusion | flops 4717568 | bytes 6496256 | tf_op jit(solution)/shard_map/reduce_sum | solution.py:37
  127.7 1.4 fusion.15
  129.1 0.8 copy-done.7
  129.9 2.0 fusion.31
  132.6 51.6 %all-reduce.3.cloned.1.call-done = f32[128,4096]{1,0:T(8,128)} async-done(((f32[128,4096]{1,0:T(8,128)}), f32[128,4096]{1,0:T(8,128)}) %all-reduce.3.cloned.1.call-update) | async-done | bytes 2097168 | tf_op jit(solution)/shard_map/psum | solution.py:106
  184.3 2.1 multiply_reduce_fusion
  187.2 13.7 %fusion.30 = (f32[128]{0:T(128)S(1)}, f32[128,4096]{1,0:T(8,128)S(1)}) fusion(bf16[4096,4096]{1,0:T(8,128)(2,1)} %param.18, f32[128,4096]{1,0:T(8,128)S(1)} %fusion.12, f32[4096]{0:T(1024)S(1)} %copy-done.8), kind=kOutput, calls=%fused_computation.69 | convolution fusion | flops 4296540160 | bytes 37765632 | tf_op jit(solution)/shard_map/dot_general | solution.py:112
  201.0 0.7 select_reduce_fusion.1
  201.7 5.0 %all-gather.5 = f32[4,1,128]{2,1,0:T(1,128)S(1)} all-gather(f32[1,1,128]{2,1,0:T(1,128)S(1)} %bitcast.72), channel_id=4, replica_groups=mesh['dp'=8,'fsdp'=4] {'fsdp'}, dimensions={0}, use_global_device_ids=true | all-gather | bytes 2560 | tf_op jit(solution)/shard_map/all_gather | solution.py:10
  206.7 5.0 %all-gather.4 = f32[4,1,128]{2,1,0:T(1,128)S(1)} all-gather(f32[1,1,128]{2,1,0:T(1,128)S(1)} %bitcast.71), channel_id=3, replica_groups=mesh['dp'=8,'fsdp'=4] {'fsdp'}, dimensions={0}, use_global_device_ids=true | all-gather | bytes 2560 | tf_op jit(solution)/shard_map/all_gather | solution.py:10
  211.8 5.2 %all-gather.3 = f32[4,1,128]{2,1,0:T(1,128)S(1)} all-gather(f32[1,1,128]{2,1,0:T(1,128)S(1)} %bitcast.69), channel_id=2, replica_groups=mesh['dp'=8,'fsdp'=4] {'fsdp'}, dimensions={0}, use_global_device_ids=true | all-gather | bytes 2560 | tf_op jit(solution)/shard_map/all_gather | solution.py:10
  217.7 17.3 %convolution_bitcast_fusion = f32[4096,128]{0,1:T(8,128)} fusion(bf16[4096,4096]{1,0:T(8,128)(2,1)} %param.18, f32[128,4096]{1,0:T(8,128)S(1)} %get-tuple-element.216, f32[128]{0:T(128)S(1)} %get-tuple-element.209, f32[128]{0:T(128)S(1)} %convert_element_type.30, s32[128]{0:T(128)S(1)} %broadcast_subtract_fusion), kind=kOutput, calls=%fused_computation.14 | convolution fusion | flops 4298113024 | bytes 37750272 | tf_op jit(solution)/shard_map/dot_general | solution.py:128
  235.0 31.7 %reduce-scatter.2.cloned.1.call-done = f32[1024,128]{0,1:T(8,128)} async-done(((f32[4096,128]{0,1:T(8,128)}), f32[1024,128]{0,1:T(8,128)}) %reduce-scatter.2.cloned.1.call-update) | async-done | bytes 524304 | tf_op jit(solution)/shard_map/reduce_scatter | solution.py:127
  266.7 1.2 fusion.21
  267.9 5.8 %psum.38 = f32[128]{0:T(128)S(1)} all-reduce(f32[128]{0:T(128)S(1)} %get-tuple-element.185), channel_id=1, replica_groups=mesh['dp'=8,'fsdp'=4] {'fsdp'}, use_global_device_ids=true, to_apply=%region_16.17 | all-reduce | flops 128 | bytes 1024 | tf_op jit(solution)/shard_map/psum | solution.py:136
  273.7 22.5 %all-reduce = (f32[]{:T(128)}, f32[]{:T(128)}, f32[1024]{0:T(1024)S(1)}) all-reduce(f32[]{:T(128)} %get-tuple-element.189, f32[]{:T(128)} %get-tuple-element.188, f32[1024]{0:T(1024)S(1)} %get-tuple-element.184), channel_id=1, replica_groups=mesh['dp'=8,'fsdp'=4] {'dp'}, use_global_device_ids=true, to_apply=%region_11.12 | all-reduce | flops 1026 | bytes 8208 | tf_op jit(solution)/shard_map/psum | solution.py:139
  296.2 1.3 broadcast_divide_fusion
  298.8 2.6 divide_convert_fusion
  (49 shorter events, 3.3 us)
Async XLA Ops:
  7.2 40.3 %copy-start = (s32[8,4]{0,1:T(4,128)S(1)}, s32[8,4]{0,1:T(4,128)}, u32[]{:S(2)}) copy-start(s32[8,4]{0,1:T(4,128)} %param.21) | copy-start | bytes 388
  7.2 177.1 %all-reduce.3.cloned.1.call-start = ((), (), s32[]{:S(2)}) async-start(), calls=%async_computation.1 | async-start | bytes 4194304 | tf_op jit(solution)/shard_map/psum | solution.py:106
  7.2 12.3 %collective-permute-start = (bf16[2,192,512]{2,1,0:T(8,128)(2,1)}, bf16[2,192,512]{2,1,0:T(8,128)(2,1)S(1)}, u32[]{:S(2)}, u32[]{:S(2)}) collective-permute-start(bf16[2,192,512]{2,1,0:T(8,128)(2,1)} %param.15), channel_id=1, source_target_pairs={{0,4},{4,0},{8,12},{12,8},{16,20},{20,16},{24,28},{28,24},{1,5},{5... | collective-permute-start | bytes 1179656 | tf_op jit(solution)/shard_map/ppermute | solution.py:87
  10.2 34.1 %copy-start.5 = (bf16[128,4096]{1,0:T(8,128)(2,1)S(1)}, bf16[128,4096]{1,0:T(8,128)(2,1)}, u32[]{:S(2)}) copy-start(bf16[128,4096]{1,0:T(8,128)(2,1)} %param.13) | copy-start | bytes 3145732
  21.0 18.9 %collective-permute-start.1 = (bf16[2,384,512]{2,1,0:T(8,128)(2,1)S(1)}, bf16[2,384,512]{2,1,0:T(8,128)(2,1)}, u32[]{:S(2)}, u32[]{:S(2)}) collective-permute-start(bf16[2,384,512]{2,1,0:T(8,128)(2,1)S(1)} %maximum_select_fusion.2), channel_id=1, source_target_pairs={{0,8},{4,12},{8,0},{12,4},{16,24},{20,28},{24,16},{28,20},{1,9},{5... | collective-permute-start | bytes 2359304 | tf_op jit(solution)/shard_map/ppermute | solution.py:87
  41.8 69.4 %collective-permute-start.2 = (bf16[2,768,512]{2,1,0:T(8,128)(2,1)S(1)}, bf16[2,768,512]{2,1,0:T(8,128)(2,1)}, u32[]{:S(2)}, u32[]{:S(2)}) collective-permute-start(bf16[2,768,512]{2,1,0:T(8,128)(2,1)S(1)} %maximum_select_fusion.1), channel_id=1, source_target_pairs={{0,16},{4,20},{8,24},{12,28},{16,0},{20,4},{24,8},{28,12},{1,17},{... | collective-permute-start | bytes 4718600 | tf_op jit(solution)/shard_map/ppermute | solution.py:87
  44.4 3.3 %copy-start.11 = (s32[128]{0:T(128)S(1)}, s32[128]{0:T(128)}, u32[]{:S(2)}) copy-start(s32[128]{0:T(128)} %param.20) | copy-start | bytes 1540
  44.4 3.4 %copy-start.9 = (s32[1536]{0:T(1024)S(1)}, s32[1536]{0:T(1024)}, u32[]{:S(2)}) copy-start(s32[1536]{0:T(1024)} %param.19) | copy-start | bytes 18436
  123.1 4.6 %copy-start.2 = (f32[8,128,1536]{2,1,0:T(8,128)S(1)}, f32[8,128,1536]{2,1,0:T(8,128)}, u32[]{:S(2)}) copy-start(f32[8,128,1536]{2,1,0:T(8,128)} %get-tuple-element.214) | copy-start | bytes 18874372
  127.7 2.2 copy-start.7
  132.0 0.7 copy-start.10
  132.0 0.7 copy-start.12
  132.0 134.7 %reduce-scatter.2.cloned.1.call-start = ((), (), s32[]{:S(2)}) async-start(), calls=%async_computation.2 | async-start | bytes 2621440 | tf_op jit(solution)/shard_map/reduce_scatter | solution.py:127
  184.3 2.2 copy-start.6
  186.5 0.7 copy-start.8
  187.2 13.8 %copy-start.3 = (f32[128,4096]{1,0:T(8,128)}, f32[128,4096]{1,0:T(8,128)S(1)}, u32[]{:S(2)}) copy-start(f32[128,4096]{1,0:T(8,128)S(1)} %fusion.12) | copy-start | bytes 6291460
  235.0 31.7 %copy-start.4 = (f32[128,4096]{1,0:T(8,128)S(1)}, f32[128,4096]{1,0:T(8,128)}, u32[]{:S(2)}) copy-start(f32[128,4096]{1,0:T(8,128)} %copy-done.3) | copy-start | bytes 6291460
  235.0 66.4 %copy-start.1 = (s32[8,4]{0,1:T(4,128)S(1)}, s32[8,4]{0,1:T(4,128)}, u32[]{:S(2)}) copy-start(s32[8,4]{0,1:T(4,128)} %param.21) | copy-start | bytes 388
Sparse Core Ops, SparseCore 0:
  132.1 52.1 all-reduce.2
  235.1 31.5 reduce-scatter.1
